TPU v7x, 32 devices: a whole 2x2x4 slice. The times are simulated.
32 devices in a mesh: groups: 2 (over x), wide: 4 (over y, core), expert: 4 (over z).
Axes of the slice: x: 2, y: 2, z: 4, core: 2. Of those that a mesh axis runs over, the one named last changes fastest.
Arguments:
- prompts: bfloat16 [8, 128, 6144], P(('groups', 'wide'), None, 'expert'), parts along dimension 0, may hold values from -6 to 6
- span_slot_owner: int32 [8], P('groups'), parts along dimension 0, may hold values from 0 to 3, as said below
- row_expert_index: int32 [768, 2], P('groups'), parts along dimension 0, may hold values from 0 to 7, all different within a row
- tile_tenant_index: int32 [6], P('groups'), parts along dimension 0, may hold values from 0 to 7
- tenant_adapter_slot: int32 [16], P('groups'), parts along dimension 0, may hold values from 0 to 7, each once
- router: bfloat16 [6144, 8], replicated, may hold values from -0.078125 to 0.078125
- gate_weight: bfloat16 [2, 6144, 16384], P(None, None, ('wide', 'expert')), may hold values from -0.078125 to 0.078125
- up_weight: bfloat16 [2, 6144, 16384], P(None, None, ('wide', 'expert')), may hold values from -0.078125 to 0.078125
- down_weight: bfloat16 [2, 16384, 6144], P(None, 'wide', 'expert'), may hold values from -0.046875 to 0.046875
- adapter_down_weight: bfloat16 [16, 2, 6144, 64], P(('groups', 'wide'), None, 'expert'), parts along dimension 0, may hold values from -0.078125 to 0.078125
- adapter_up_weight: bfloat16 [16, 2, 64, 16384], P('groups', None, None, ('wide', 'expert')), parts along dimension 0, may hold values from -0.75 to 0.75
Outputs:
- mixed: bfloat16 [768, 6144], P(('groups', 'wide'), 'expert'), parts along dimension 0
There are 2 independent parts, one for each index of `groups`. A program takes and returns all parts, laid end to end along the dimension named above; an argument that names none is the same for every part. Nothing has to cross between parts.
Inputs may be any that keep to these rules, and one draw needn't show every extreme that they name: `span_slot_owner`: a permutation of the slots; span c, for c < 3, is in slot span_slot_owner[c]. `row_expert_index`: each row names two different experts. `tenant_adapter_slot`: a permutation of the slots. `tile_tenant_index`: tenant of rows 128 * i to 128 * i + 127.
All inputs are finite; a program needn't handle non-finite values.
Results may differ from a plain program's by a relative error of at most 0.0051.
Values may be sent and summed in bfloat16 or wider, within the bound.
No kernel may reach another device: no remote copies, remote signals or barrier semaphores. Data moves between devices by JAX's collectives and lax.ppermute only.
A program may use at most 128 MiB of HBM per device.

v0:
```python
import jax
import jax.numpy as jnp
from jax import lax
from jax.sharding import PartitionSpec as P

NCHUNK = 3
ADAPTER_SCALE = 0.5


def spread(block, axis, source):
    block = jnp.where(lax.axis_index(axis) == source, block, jnp.zeros_like(block))
    return lax.psum(block, axis)


def per_device(
    prompts,
    span_slot_owner,
    row_expert_index,
    tile_tenant_index,
    tenant_adapter_slot,
    router,
    gate_weight,
    up_weight,
    down_weight,
    adapter_down_weight,
    adapter_up_weight,
):
    column = lax.axis_index("expert")
    own_slot = prompts[0]
    width_part = own_slot.shape[1]
    full_slot = lax.all_gather(own_slot, "expert", axis=1, tiled=True)
    pieces = [
        spread(full_slot, "wide", span_slot_owner[span_index]) for span_index in range(NCHUNK)
    ]
    input_rows = jnp.concatenate(pieces, axis=0)
    slices = lax.dynamic_slice_in_dim(input_rows, column * width_part, width_part, 1)
    tokens = input_rows.shape[0]
    window = gate_weight.shape[0]
    logits = jnp.dot(input_rows, router, preferred_element_type=jnp.float32)
    experts = jnp.arange(router.shape[1], dtype=jnp.int32)
    picked = (row_expert_index[:, :, None] == experts[None, None, :]).astype(jnp.float32)
    chosen = jnp.sum(picked * logits[:, None, :], axis=2)
    first_prob = jax.nn.sigmoid(chosen[:, 0] - chosen[:, 1])
    second_prob = jax.nn.sigmoid(chosen[:, 1] - chosen[:, 0])
    weight = (
        first_prob[:, None] * picked[:, 0, :window] + second_prob[:, None] * picked[:, 1, :window]
    )
    tile_count = tile_tenant_index.shape[0]
    tile_rows = tokens // tile_count
    resident_slots = adapter_down_weight.shape[0]
    tile_slot_index = jnp.take(tenant_adapter_slot, tile_tenant_index)
    owners = tile_slot_index // resident_slots
    local_expert_index = tile_slot_index % resident_slots
    tile_slices = slices.reshape(tile_count, tile_rows, width_part)

    def fetch_one(state_carry, tile_position):
        adapter_piece = lax.dynamic_index_in_dim(
            adapter_down_weight, local_expert_index[tile_position], 0, keepdims=False
        )
        return (state_carry, spread(adapter_piece, "wide", owners[tile_position]))

    unused, fetched = lax.scan(fetch_one, jnp.int32(0), jnp.arange(tile_count, dtype=jnp.int32))
    partial_rank = jnp.einsum(
        "ntd,nedr->nter", tile_slices, fetched, preferred_element_type=jnp.float32
    )
    summed = lax.psum(partial_rank, "expert")
    lowrank = summed.astype(jnp.bfloat16)
    tenant_list = adapter_up_weight.shape[0]
    select_tenant = (
        tile_tenant_index[:, None] == jnp.arange(tenant_list, dtype=jnp.int32)[None, :]
    ).astype(adapter_up_weight.dtype)
    tile_up = jnp.einsum(
        "cj,jvqz->cvqz", select_tenant, adapter_up_weight, preferred_element_type=jnp.float32
    ).astype(jnp.bfloat16)
    adapted_hidden = jnp.einsum(
        "nter,nerf->ntef", lowrank, tile_up, preferred_element_type=jnp.float32
    )
    adapted_hidden = adapted_hidden.reshape(tokens, window, adapted_hidden.shape[3])
    gate_pre = jnp.einsum(
        "td,edf->tef", input_rows, gate_weight, preferred_element_type=jnp.float32
    )
    up_projection_value = (
        jnp.einsum("td,edf->tef", input_rows, up_weight, preferred_element_type=jnp.float32)
        + ADAPTER_SCALE * adapted_hidden
    )
    hidden = (weight[:, :, None] * jax.nn.silu(gate_pre) * up_projection_value).astype(jnp.bfloat16)
    partial_out = jnp.einsum(
        "tef,efd->td",
        lax.all_gather(hidden, "expert", axis=2, tiled=True),
        down_weight,
        preferred_element_type=jnp.float32,
    )
    mixed_rows = lax.psum_scatter(partial_out, "wide", scatter_dimension=0, tiled=True)
    return mixed_rows.astype(jnp.bfloat16)


def solution(mesh):
    in_specs = (
        P(("groups", "wide"), None, "expert"),
        P("groups"),
        P("groups", None),
        P("groups"),
        P("groups"),
        P(),
        P(None, None, ("wide", "expert")),
        P(None, None, ("wide", "expert")),
        P(None, "wide", "expert"),
        P(("groups", "wide"), None, "expert", None),
        P("groups", None, None, ("wide", "expert")),
    )
    out_specs = P(("groups", "wide"), "expert")
    return jax.shard_map(
        per_device, mesh=mesh, in_specs=in_specs, out_specs=out_specs, check_vma=False
    )
```

profile of v0, /device:TPU:0, one launch (start us, length us, event | category | flops | bytes accessed | tf_op | source)
XLA Modules:
  0.0 514.7 jit_solution(17569741497082177469)
XLA Ops:
  6.5 0.0 copy-start
  6.5 0.0 all-gather.6.cloned.1.call-start
  6.5 0.7 all-gather.6.cloned.1.call-update
  7.3 0.0 all-reduce.5.cloned.1.call-start
  7.3 1.4 fusion.18
  10.5 38.3 %all-gather.6.cloned.1.call-done = bf16[1,128,6144]{2,1,0:T(8,128)(2,1)} async-done(((bf16[1,128,1536]{2,1,0:T(8,128)(2,1)}), bf16[1,128,6144]{2,1,0:T(8,128)(2,1)}) %all-gather.6.cloned.1.call-update) | async-done | bytes 1572880 | tf_op jit(solution)/shard_map/all_gather | solution.py:31
  48.8 3.7 select_bitcast_fusion
  52.4 0.0 all-reduce.5.cloned.1.call-update
  52.5 0.6 copy-done.10
  53.1 0.0 copy-done.2
  53.1 0.6 gather_fusion
  53.8 0.0 copy-done.9
  53.8 2.5 fusion.6
  56.3 89.6 %all-reduce.5.cloned.1.call-done = (bf16[128,6144]{1,0:T(8,128)(2,1)}, bf16[128,6144]{1,0:T(8,128)(2,1)}, bf16[128,6144]{1,0:T(8,128)(2,1)}) async-done(((bf16[128,6144]{1,0:T(8,128)(2,1)}, bf16[128,6144]{1,0:T(8,128)(2,1)}, bf16[128,6144]{1,0:T(8,128)(2,1)}), (bf16[128,6144]{1,0:T(8,128)(2,1)}, bf16[128,6144]{1,0:T(8,128)(2,1)}, bf16[128,6144]{1,0:T(8,128)(2,1)})) %all-reduce.5.cloned.1.call-update) | async-done | bytes 4718608 | tf_op jit(solution)/shard_map/psum | solution.py:12
  145.9 1.7 constant_dynamic-update-slice_fusion.3
  147.5 0.2 copy-done.7
  147.8 0.1 constant_dynamic-update-slice_fusion.2
  147.9 0.3 copy-done.6
  148.2 0.1 constant_dynamic-update-slice_fusion.1
  148.4 0.4 copy-done.8
  148.8 1.3 fusion.19
  150.2 0.1 constant_dynamic-slice_fusion.1
  150.3 0.6 copy-done.3
  150.9 134.1 %while.10 = (s32[]{:T(128)}, bf16[3,2,1536,64]{3,2,1,0:T(8,128)(2,1)}, s32[3]{0:T(128)S(1)}, s32[3]{0:T(128)S(1)}, s32[3]{0:T(128)S(1)}, /*index=5*/bf16[2,2,153...) while((s32[]{:T(128)}, ...), condition=%wide.region_6.7_spmd, body=%wide.region_4.6_spmd.sunk | while | flops 393228 | bytes 7078207 | solution.py:62
  150.9 0.6 dynamic_slice.25
  153.4 0.6 dynamic_slice.26
  156.0 0.4 copy.26
  156.4 0.6 dynamic_slice.27
  157.6 1.0 broadcast_select_fusion.2
  158.6 0.0 all-reduce.7.cloned.1.call-update
  158.7 34.9 %all-reduce.7.cloned.1.call-done = bf16[1,2,1536,64]{3,2,1,0:T(8,128)(2,1)} async-done(((bf16[1,2,1536,64]{3,2,1,0:T(8,128)(2,1)}), bf16[1,2,1536,64]{3,2,1,0:T(8,128)(2,1)}) %all-reduce.7.cloned.1.call-update) | async-done | bytes 393232 | tf_op jit(solution)/shard_map/while/body/eval_jaxpr/psum | solution.py:12
  193.6 2.1 constant_dynamic-update-slice_fusion.5
  195.7 0.6 dynamic_slice.25
  198.2 0.6 dynamic_slice.26
  200.8 0.4 copy.26
  201.1 0.6 dynamic_slice.27
  202.4 1.0 broadcast_select_fusion.2
  203.4 0.0 all-reduce.7.cloned.1.call-update
  203.4 34.8 %all-reduce.7.cloned.1.call-done = bf16[1,2,1536,64]{3,2,1,0:T(8,128)(2,1)} async-done(((bf16[1,2,1536,64]{3,2,1,0:T(8,128)(2,1)}), bf16[1,2,1536,64]{3,2,1,0:T(8,128)(2,1)}) %all-reduce.7.cloned.1.call-update) | async-done | bytes 393232 | tf_op jit(solution)/shard_map/while/body/eval_jaxpr/psum | solution.py:12
  238.2 2.1 constant_dynamic-update-slice_fusion.5
  240.3 0.6 dynamic_slice.25
  242.8 0.6 dynamic_slice.26
  245.4 0.4 copy.26
  245.8 0.6 dynamic_slice.27
  247.0 1.0 broadcast_select_fusion.2
  248.0 0.0 all-reduce.7.cloned.1.call-update
  248.1 34.8 %all-reduce.7.cloned.1.call-done = bf16[1,2,1536,64]{3,2,1,0:T(8,128)(2,1)} async-done(((bf16[1,2,1536,64]{3,2,1,0:T(8,128)(2,1)}), bf16[1,2,1536,64]{3,2,1,0:T(8,128)(2,1)}) %all-reduce.7.cloned.1.call-update) | async-done | bytes 393232 | tf_op jit(solution)/shard_map/while/body/eval_jaxpr/psum | solution.py:12
  282.9 2.1 constant_dynamic-update-slice_fusion.5
  285.0 2.6 fusion.20
  287.6 22.5 %all-reduce.8 = bf16[3,128,2,64]{1,3,2,0:T(8,128)(2,1)S(1)} all-reduce(f32[3,128,2,64]{1,3,2,0:T(8,128)S(1)} %fusion.20), channel_id=1, replica_groups=mesh['groups'=2,'wide'=4,'expert'=4] {'expert'}, use_global_device_ids=true, to_apply=%region_7.8 | all-reduce | flops 49152 | bytes 294912 | tf_op jit(solution)/shard_map/psum | solution.py:66
  310.1 0.0 slice-start.1
  310.1 0.8 multiply_bitcast_fusion
  310.8 0.2 copy.15
  311.1 1.2 slice-done.1
  312.2 15.1 %fusion.2 = f32[384,2,1024]{2,0,1:T(8,128)} fusion(bf16[2,6144,1024]{2,1,0:T(8,128)(2,1)} %param.19, bf16[384,6144]{1,0:T(8,128)(2,1)S(1)} %bitcast.68), kind=kOutput, calls=%fused_computation.6 | convolution fusion | flops 9663676416 | bytes 33030144 | tf_op jit(solution)/shard_map/td,edf->tef/dot_general | solution.py:79
  327.4 16.2 %fusion.5 = bf16[384,2,1024]{2,0,1:T(8,128)(2,1)} fusion(f32[3,128,2,1024]{3,1,0,2:T(8,128)S(1)} %copy.15, f32[384,2,1024]{2,0,1:T(8,128)} %fusion.2, f32[384,2]{0,1:T(2,128)S(1)} %fusion.13, bf16[2,6144,1024]{2,1,0:T(8,128)(2,1)} %param.20, bf16[384,6144]{1,0:T(8,128)(2,1)S(1)} %bitcast.68), kind=kOutput, calls=%fused_computation.10 | convolution fusion | flops 9669967872 | bytes 37751808 | tf_op jit(solution)/shard_map/td,edf->tef/dot_general | solution.py:83
  343.6 0.0 all-gather.4.cloned.1.call-update
  343.6 0.0 reduce-scatter.2.cloned.1.call-start
  343.7 113.3 %all-gather.4.cloned.1.call-done = bf16[384,2,4096]{2,0,1:T(8,128)(2,1)} async-done(((bf16[384,2,1024]{2,0,1:T(8,128)(2,1)}), bf16[384,2,4096]{2,0,1:T(8,128)(2,1)}) %all-gather.4.cloned.1.call-update) | async-done | bytes 6291472 | tf_op jit(solution)/shard_map/all_gather | solution.py:89
  456.9 17.7 %convolution_bitcast_fusion = f32[384,1536]{1,0:T(8,128)} fusion(bf16[384,2,4096]{2,0,1:T(8,128)(2,1)} %all-gather.4.cloned.1.call-done, bf16[2,4096,1536]{2,1,0:T(8,128)(2,1)} %param.21), kind=kOutput, calls=%fused_computation.12 | convolution fusion | flops 9663676416 | bytes 33816576 | tf_op jit(solution)/shard_map/tef,efd->td/dot_general | solution.py:87
  474.6 0.0 reduce-scatter.2.cloned.1.call-update
  474.6 31.4 %reduce-scatter.2.cloned.1.call-done = f32[96,1536]{1,0:T(8,128)} async-done(((f32[384,1536]{1,0:T(8,128)}), f32[96,1536]{1,0:T(8,128)}) %reduce-scatter.2.cloned.1.call-update) | async-done | bytes 589840 | tf_op jit(solution)/shard_map/reduce_scatter | solution.py:93
  506.0 1.8 convert_element_type.20
  507.8 0.0 copy-done.1
  (33 shorter events, 0.3 us)
Async XLA Ops:
  6.5 47.3 %copy-start = (bf16[8,2,64,1024]{3,2,1,0:T(8,128)(2,1)S(1)}, bf16[8,2,64,1024]{3,2,1,0:T(8,128)(2,1)}, u32[]{:S(2)}) copy-start(bf16[8,2,64,1024]{3,2,1,0:T(8,128)(2,1)} %param.23) | copy-start | bytes 6291460
  6.5 42.2 %all-gather.6.cloned.1.call-start = ((), (), s32[]{:S(2)}) async-start(), calls=%async_computation.3 | async-start | bytes 1966080 | tf_op jit(solution)/shard_map/all_gather | solution.py:31
  7.3 138.6 %all-reduce.5.cloned.1.call-start = ((), (), s32[]{:S(2)}) async-start(), calls=%async_computation.4 | async-start | bytes 9437184 | tf_op jit(solution)/shard_map/psum | solution.py:12
  52.4 0.7 copy-start.10
  52.4 0.7 copy-start.2
  52.4 1.3 copy-start.9
  145.9 1.9 copy-start.7
  145.9 2.4 copy-start.6
  147.8 1.0 copy-start.8
  148.8 2.1 copy-start.3
  148.8 2.1 copy-start.4
  150.9 42.7 %all-reduce.7.cloned.1.call-start = ((), (), s32[]{:S(2)}) async-start(), calls=%async_computation.5 | async-start | bytes 1572864 | tf_op jit(solution)/shard_map/while/body/eval_jaxpr/psum | solution.py:12
  195.7 42.6 %all-reduce.7.cloned.1.call-start = ((), (), s32[]{:S(2)}) async-start(), calls=%async_computation.5 | async-start | bytes 1572864 | tf_op jit(solution)/shard_map/while/body/eval_jaxpr/psum | solution.py:12
  240.3 42.6 %all-reduce.7.cloned.1.call-start = ((), (), s32[]{:S(2)}) async-start(), calls=%async_computation.5 | async-start | bytes 1572864 | tf_op jit(solution)/shard_map/while/body/eval_jaxpr/psum | solution.py:12
  285.0 25.1 %copy-start.5 = (bf16[3,2,64,1024]{3,0,2,1:T(4,128)(2,1)S(1)}, bf16[3,2,64,1024]{3,0,2,1:T(4,128)(2,1)}, u32[]{:S(2)}) copy-start(bf16[3,2,64,1024]{3,0,2,1:T(4,128)(2,1)} %fusion.6) | copy-start | bytes 2359300
  285.0 171.9 %all-gather.4.cloned.1.call-start = ((), (), s32[]{:S(2)}) async-start(), calls=%async_computation.1 | async-start | bytes 7864320 | tf_op jit(solution)/shard_map/all_gather | solution.py:89
  285.0 26.1 %slice-start = ((s8[4718592]{0:T(1024)(128)(4,1)}), s8[524288]{0:T(1024)(128)(4,1)S(1)}, s32[]{:S(2)}) async-start(s8[4718592]{0:T(1024)(128)(4,1)} %bitcast.67), calls=%async_computation.6 | async-start | bytes 1048576
  310.1 2.2 slice-start.1
  343.6 162.4 %reduce-scatter.2.cloned.1.call-start = ((), (), s32[]{:S(2)}) async-start(), calls=%async_computation.2 | async-start | bytes 2949120 | tf_op jit(solution)/shard_map/reduce_scatter | solution.py:93
  456.9 50.9 %copy-start.1 = (bf16[8,2,64,1024]{3,2,1,0:T(8,128)(2,1)S(1)}, bf16[8,2,64,1024]{3,2,1,0:T(8,128)(2,1)}, u32[]{:S(2)}) copy-start(bf16[8,2,64,1024]{3,2,1,0:T(8,128)(2,1)} %param.23) | copy-start | bytes 6291460
Sparse Core Ops, SparseCore 0:
  8.9 39.7 all-gather.5
  52.6 93.2 all-reduce.4
  158.8 34.7 all-reduce.6
  203.5 34.6 all-reduce.6
  248.2 34.6 all-reduce.6
  343.7 113.1 all-gather.3
  474.7 31.2 reduce-scatter.1
where the time goes:
time: 515 us
  waiting for transfers between devices  378 us (73%)
  matrix products  56.1 us (11%)
  blocking collectives  22.5 us (4%)
  local copies, waits for them, and re-layouts  20.4 us (4%)
  between operations  15.4 us (3%)
  loops' own time  13.7 us (3%)
  other arithmetic  8.61 us (2%)
    psum x4, waiting for transfers between devices, spread(): return lax.psum(block, axis)  194 us
    all_gather x1, waiting for transfers between devices, per_device(): lax.all_gather(hidden, 'expert', axis=2, tiled=True)  113 us
    all_gather x1, waiting for transfers between devices, per_device(): full_slot = lax.all_gather(own_slot, 'expert', axis=1, tiled=True)  38.3 us
    reduce_scatter x1, waiting for transfers between devices, per_device(): lax.psum_scatter(partial_out, 'wide', scatter_dimension=0, tiled=True)  31.4 us
    psum x1, blocking collectives, per_device(): summed = lax.psum(partial_rank, 'expert')  22.5 us
    dot_general x1, matrix products, per_device(): jnp.einsum('tef,efd->td', lax.all_gather(hidden, 'expert', axis=2, tiled=...  17.7 us
    dot_general x1, matrix products, per_device(): jnp.einsum('td,edf->tef', input_rows, up_weight, preferred_element_type=j...  16.2 us
    dot_general x1, matrix products, per_device(): jnp.einsum('td,edf->tef', input_rows, gate_weight, preferred_element_type...  15.1 us
  transfers between devices with their start and end apart: 7, of which 7 were waited for; matrix products, arithmetic and copies ran while one was open for 1% of the time, Pallas kernels for 0%

commit v1 on v0

--- a/solution.py
+++ b/solution.py
@@ -2,6 +2,7 @@
 import jax.numpy as jnp
 from jax import lax
 from jax.sharding import PartitionSpec as P
+from jax.lax import axis_index, axis_size, ppermute
 
 NCHUNK = 3
 ADAPTER_SCALE = 0.5
@@ -84,12 +85,44 @@
         + ADAPTER_SCALE * adapted_hidden
     )
     hidden = (weight[:, :, None] * jax.nn.silu(gate_pre) * up_projection_value).astype(jnp.bfloat16)
+    val = axis_size("expert")
+    passed = axis_index("expert")
+    e_next, block_last, current_block = (val, passed, hidden.shape[2])
+    cards = tuple(((k0, (k0 + 1) % e_next) for k0 in range(e_next)))
+    z2 = e_next // 2
+    rows = tuple(((k0, (k0 - 1) % e_next) for k0 in range(e_next)))
     partial_out = jnp.einsum(
         "tef,efd->td",
-        lax.all_gather(hidden, "expert", axis=2, tiled=True),
-        down_weight,
+        hidden,
+        lax.dynamic_slice_in_dim(down_weight, block_last * current_block, hidden.shape[2], axis=1),
         preferred_element_type=jnp.float32,
     )
+    vec_out = tile_out = hidden
+    for no in tuple(range(1, z2 + 1)):
+        vec_out = ppermute(vec_out, "expert", cards)
+        if no < e_next - z2:
+            tile_out = ppermute(tile_out, "expert", rows)
+            carry_out = jnp.einsum(
+                "tef,efd->td",
+                tile_out,
+                lax.dynamic_slice_in_dim(
+                    down_weight,
+                    (block_last + no) % e_next * current_block,
+                    tile_out.shape[2],
+                    axis=1,
+                ),
+                preferred_element_type=jnp.float32,
+            )
+            partial_out = partial_out + carry_out
+        extra = jnp.einsum(
+            "tef,efd->td",
+            vec_out,
+            lax.dynamic_slice_in_dim(
+                down_weight, (block_last - no) % e_next * current_block, vec_out.shape[2], axis=1
+            ),
+            preferred_element_type=jnp.float32,
+        )
+        partial_out = partial_out + extra
     mixed_rows = lax.psum_scatter(partial_out, "wide", scatter_dimension=0, tiled=True)
     return mixed_rows.astype(jnp.bfloat16)
 

time: 515 us -> 492 us (0.955)
  waiting for transfers between devices: 378 us -> 319 us
  starting transfers between devices: 0.09 us -> 30.6 us
    all_gather x1 -> x0, waiting for transfers between devices: 113 us -> none  [per_device(): lax.all_gather(hidden, 'expert', axis=2, tiled=True)]
    ppermute x0 -> x3, waiting for transfers between devices: none -> 55.5 us  [the longest x2 55.5 us: per_device(): vec_out = ppermute(vec_out, 'expert', cards)]
    ppermute x0 -> x3, starting transfers between devices: none -> 30.6 us  [the longest x2 26.8 us: per_device(): vec_out = ppermute(vec_out, 'expert', cards)]
    dot_general x1 -> x4, matrix products: 17.7 us -> 21.7 us  [the longest x2 11.8 us: per_device(): jnp.einsum('tef,efd->td', vec_out, lax.dynamic_slice_in_dim(down_weight,...]
  transfers between devices with their start and end apart: 7 -> 9, of which waited for: 7 -> 8; matrix products, arithmetic and copies ran while one was open for 1% -> 4% of each run, Pallas kernels for 0% -> 0%
where the time goes in v1:
time: 492 us; the launch traced here: 491 us
  waiting for transfers between devices  319 us (65%)
  matrix products  59.2 us (12%)
  starting transfers between devices  30.6 us (6%)
  blocking collectives  22.5 us (5%)
  local copies, waits for them, and re-layouts  21.3 us (4%)
  between operations  15.5 us (3%)
  loops' own time  13.7 us (3%)
  other arithmetic  8.61 us (2%)
    psum x4, waiting for transfers between devices, spread(): return lax.psum(block, axis)  194 us
    ppermute x2, waiting for transfers between devices, per_device(): vec_out = ppermute(vec_out, 'expert', cards)  55.5 us
    all_gather x1, waiting for transfers between devices, per_device(): full_slot = lax.all_gather(own_slot, 'expert', axis=1, tiled=True)  38.3 us
    reduce_scatter x1, waiting for transfers between devices, per_device(): lax.psum_scatter(partial_out, 'wide', scatter_dimension=0, tiled=True)  30.8 us
    ppermute x2, starting transfers between devices, per_device(): vec_out = ppermute(vec_out, 'expert', cards)  26.8 us
    psum x1, blocking collectives, per_device(): summed = lax.psum(partial_rank, 'expert')  22.5 us
    dot_general x1, matrix products, per_device(): jnp.einsum('td,edf->tef', input_rows, up_weight, preferred_element_type=j...  15.3 us
    dot_general x1, matrix products, per_device(): jnp.einsum('td,edf->tef', input_rows, gate_weight, preferred_element_type...  15.1 us
  transfers between devices with their start and end apart: 9, of which 8 were waited for; matrix products, arithmetic and copies ran while one was open for 4% of the time, Pallas kernels for 0%

profile of v1, /device:TPU:0, one launch (start us, length us, event | category | flops | bytes accessed | tf_op | source)
XLA Modules:
  0.0 490.9 jit_solution(393987715352088893)
XLA Ops:
  6.5 0.7 all-gather.3.cloned.1.call-update
  7.3 0.0 all-reduce.5.cloned.1.call-start
  7.3 1.4 fusion.51
  10.5 38.3 %all-gather.3.cloned.1.call-done = bf16[1,128,6144]{2,1,0:T(8,128)(2,1)} async-done(((bf16[1,128,1536]{2,1,0:T(8,128)(2,1)}), bf16[1,128,6144]{2,1,0:T(8,128)(2,1)}) %all-gather.3.cloned.1.call-update) | async-done | bytes 1572880 | tf_op jit(solution)/shard_map/all_gather | solution.py:32
  48.8 3.7 select_bitcast_fusion
  52.4 0.0 all-reduce.5.cloned.1.call-update
  52.5 0.6 copy-done.10
  53.1 0.6 gather_fusion
  53.8 2.5 fusion.35
  56.3 89.6 %all-reduce.5.cloned.1.call-done = (bf16[128,6144]{1,0:T(8,128)(2,1)}, bf16[128,6144]{1,0:T(8,128)(2,1)}, bf16[128,6144]{1,0:T(8,128)(2,1)}) async-done(((bf16[128,6144]{1,0:T(8,128)(2,1)}, bf16[128,6144]{1,0:T(8,128)(2,1)}, bf16[128,6144]{1,0:T(8,128)(2,1)}), (bf16[128,6144]{1,0:T(8,128)(2,1)}, bf16[128,6144]{1,0:T(8,128)(2,1)}, bf16[128,6144]{1,0:T(8,128)(2,1)})) %all-reduce.5.cloned.1.call-update) | async-done | bytes 4718608 | tf_op jit(solution)/shard_map/psum | solution.py:13
  145.9 1.6 constant_dynamic-update-slice_fusion.3
  147.5 0.2 copy-done.7
  147.8 0.1 constant_dynamic-update-slice_fusion.2
  147.9 0.0 copy-start.8
  147.9 1.1 copy-done.6
  149.0 0.1 constant_dynamic-update-slice_fusion.1
  149.1 1.3 fusion.52
  150.5 0.7 copy-done.3
  151.3 0.1 constant_dynamic-slice_fusion.1
  151.4 0.5 copy-done.4
  151.9 134.1 %while.10 = (s32[]{:T(128)}, bf16[3,2,1536,64]{3,2,1,0:T(8,128)(2,1)}, s32[3]{0:T(128)S(1)}, s32[3]{0:T(128)S(1)}, s32[3]{0:T(128)S(1)}, /*index=5*/bf16[2,2,153...) while((s32[]{:T(128)}, ...), condition=%wide.region_6.7_spmd, body=%wide.region_4.6_spmd.sunk | while | flops 393228 | bytes 7078207 | solution.py:63
  151.9 0.6 dynamic_slice.63
  154.4 0.6 dynamic_slice.64
  157.0 0.4 copy.26
  157.3 0.6 dynamic_slice.65
  158.6 1.0 broadcast_select_fusion.2
  159.6 0.0 all-reduce.7.cloned.1.call-update
  159.6 34.9 %all-reduce.7.cloned.1.call-done = bf16[1,2,1536,64]{3,2,1,0:T(8,128)(2,1)} async-done(((bf16[1,2,1536,64]{3,2,1,0:T(8,128)(2,1)}), bf16[1,2,1536,64]{3,2,1,0:T(8,128)(2,1)}) %all-reduce.7.cloned.1.call-update) | async-done | bytes 393232 | tf_op jit(solution)/shard_map/while/body/eval_jaxpr/psum | solution.py:13
  194.5 2.1 constant_dynamic-update-slice_fusion.5
  196.6 0.6 dynamic_slice.63
  199.1 0.6 dynamic_slice.64
  201.7 0.4 copy.26
  202.1 0.6 dynamic_slice.65
  203.3 1.0 broadcast_select_fusion.2
  204.3 0.0 all-reduce.7.cloned.1.call-update
  204.4 34.8 %all-reduce.7.cloned.1.call-done = bf16[1,2,1536,64]{3,2,1,0:T(8,128)(2,1)} async-done(((bf16[1,2,1536,64]{3,2,1,0:T(8,128)(2,1)}), bf16[1,2,1536,64]{3,2,1,0:T(8,128)(2,1)}) %all-reduce.7.cloned.1.call-update) | async-done | bytes 393232 | tf_op jit(solution)/shard_map/while/body/eval_jaxpr/psum | solution.py:13
  239.2 2.1 constant_dynamic-update-slice_fusion.5
  241.3 0.6 dynamic_slice.63
  243.8 0.6 dynamic_slice.64
  246.4 0.4 copy.26
  246.7 0.6 dynamic_slice.65
  248.0 1.0 broadcast_select_fusion.2
  249.0 0.0 all-reduce.7.cloned.1.call-update
  249.0 34.8 %all-reduce.7.cloned.1.call-done = bf16[1,2,1536,64]{3,2,1,0:T(8,128)(2,1)} async-done(((bf16[1,2,1536,64]{3,2,1,0:T(8,128)(2,1)}), bf16[1,2,1536,64]{3,2,1,0:T(8,128)(2,1)}) %all-reduce.7.cloned.1.call-update) | async-done | bytes 393232 | tf_op jit(solution)/shard_map/while/body/eval_jaxpr/psum | solution.py:13
  283.8 2.1 constant_dynamic-update-slice_fusion.5
  285.9 2.6 fusion.53
  288.5 22.5 %all-reduce.8 = bf16[3,128,2,64]{1,3,2,0:T(8,128)(2,1)S(1)} all-reduce(f32[3,128,2,64]{1,3,2,0:T(8,128)S(1)} %fusion.53), channel_id=1, replica_groups=mesh['groups'=2,'wide'=4,'expert'=4] {'expert'}, use_global_device_ids=true, to_apply=%region_7.8 | all-reduce | flops 49152 | bytes 294912 | tf_op jit(solution)/shard_map/psum | solution.py:67
  311.0 0.8 multiply_bitcast_fusion
  311.8 0.2 copy.15
  312.0 1.2 slice-done.1
  313.2 15.1 %fusion.10 = f32[384,2,1024]{2,0,1:T(8,128)} fusion(bf16[2,6144,1024]{2,1,0:T(8,128)(2,1)} %param.19, bf16[384,6144]{1,0:T(8,128)(2,1)S(1)} %bitcast.82), kind=kOutput, calls=%fused_computation.14 | convolution fusion | flops 9663676416 | bytes 33030144 | tf_op jit(solution)/shard_map/td,edf->tef/dot_general | solution.py:80
  328.3 15.3 %fusion.13 = bf16[384,2,1024]{2,0,1:T(8,128)(2,1)S(1)} fusion(f32[3,128,2,1024]{3,1,0,2:T(8,128)S(1)} %copy.15, f32[384,2,1024]{2,0,1:T(8,128)} %fusion.10, f32[384,2]{0,1:T(2,128)S(1)} %fusion.42, bf16[2,6144,1024]{2,1,0:T(8,128)(2,1)} %param.20, bf16[384,6144]{1,0:T(8,128)(2,1)S(1)} %bitcast.82), kind=kOutput, calls=%fused_computation.18 | convolution fusion | flops 9669967872 | bytes 37751808 | tf_op jit(solution)/shard_map/td,edf->tef/dot_general | solution.py:84
  343.7 0.1 collective-permute-start.1
  343.7 3.8 collective-permute-start
  347.5 35.3 %collective-permute-done.1 = bf16[384,2,1024]{2,0,1:T(8,128)(2,1)S(1)} collective-permute-done((bf16[384,2,1024]{2,0,1:T(8,128)(2,1)S(1)}, bf16[384,2,1024]{2,0,1:T(8,128)(2,1)S(1)}, u32[]{:S(2)}, u32[]{:S(2)}) %collective-permute-start.1) | collective-permute-done | bytes 1572896 | tf_op jit(solution)/shard_map/ppermute | solution.py:102
  382.8 26.7 %collective-permute-start.2 = (bf16[384,2,1024]{2,0,1:T(8,128)(2,1)S(1)}, bf16[384,2,1024]{2,0,1:T(8,128)(2,1)S(1)}, u32[]{:S(2)}, u32[]{:S(2)}) collective-permute-start(bf16[384,2,1024]{2,0,1:T(8,128)(2,1)S(1)} %collective-permute-done.1), channel_id=1, source_target_pairs={{0,1},{1,2},{2,3},{3,0},{4,5},{5,6},{6,7},{7,4},{8,9},{9,10},{10,1... | collective-permute-start | bytes 4718600 | tf_op jit(solution)/shard_map/ppermute | solution.py:102
  409.5 4.7 fusion.14
  414.3 5.2 %fusion.32 = f32[384,1536]{1,0:T(8,128)S(1)} fusion(f32[384,1536]{1,0:T(8,128)S(1)} %fusion.14, bf16[384,2,1024]{2,0,1:T(8,128)(2,1)} %collective-permute-done, bf16[2,4096,1536]{2,1,0:T(8,128)(2,1)} %param.21, s32[]{:T(128)S(6)} %select_n.101), kind=kOutput, calls=%fused_computation.26 | convolution fusion | flops 2416508928 | bytes 12582916 | tf_op jit(solution)/shard_map/tef,efd->td/dot_general | solution.py:105
  419.5 4.7 fusion.29
  424.2 20.2 %collective-permute-done.2 = bf16[384,2,1024]{2,0,1:T(8,128)(2,1)S(1)} collective-permute-done((bf16[384,2,1024]{2,0,1:T(8,128)(2,1)S(1)}, bf16[384,2,1024]{2,0,1:T(8,128)(2,1)S(1)}, u32[]{:S(2)}, u32[]{:S(2)}) %collective-permute-start.2) | collective-permute-done | bytes 1572896 | tf_op jit(solution)/shard_map/ppermute | solution.py:102
  444.5 7.0 %fusion.26 = f32[384,1536]{1,0:T(8,128)} fusion(f32[384,1536]{1,0:T(8,128)S(1)} %fusion.29, bf16[384,2,1024]{2,0,1:T(8,128)(2,1)S(1)} %collective-permute-done.2, bf16[2,4096,1536]{2,1,0:T(8,128)(2,1)} %param.21, s32[]{:T(128)S(6)} %select_n.105), kind=kOutput, calls=%fused_computation.24 | convolution fusion | flops 2416508928 | bytes 12582916 | tf_op jit(solution)/shard_map/tef,efd->td/dot_general | solution.py:117
  451.5 0.0 reduce-scatter.2.cloned.1.call-update
  451.5 30.8 %reduce-scatter.2.cloned.1.call-done = f32[96,1536]{1,0:T(8,128)} async-done(((f32[384,1536]{1,0:T(8,128)}), f32[96,1536]{1,0:T(8,128)}) %reduce-scatter.2.cloned.1.call-update) | async-done | bytes 589840 | tf_op jit(solution)/shard_map/reduce_scatter | solution.py:126
  482.3 1.8 convert_element_type.20
  (39 shorter events, 0.3 us)
Async XLA Ops:
  6.5 47.3 %copy-start = (bf16[8,2,64,1024]{3,2,1,0:T(8,128)(2,1)S(1)}, bf16[8,2,64,1024]{3,2,1,0:T(8,128)(2,1)}, u32[]{:S(2)}) copy-start(bf16[8,2,64,1024]{3,2,1,0:T(8,128)(2,1)} %param.23) | copy-start | bytes 6291460
  6.5 42.2 %all-gather.3.cloned.1.call-start = ((), (), s32[]{:S(2)}) async-start(), calls=%async_computation.2 | async-start | bytes 1966080 | tf_op jit(solution)/shard_map/all_gather | solution.py:32
  7.3 138.6 %all-reduce.5.cloned.1.call-start = ((), (), s32[]{:S(2)}) async-start(), calls=%async_computation.3 | async-start | bytes 9437184 | tf_op jit(solution)/shard_map/psum | solution.py:13
  52.4 0.7 copy-start.10
  52.4 0.7 copy-start.2
  52.4 1.3 copy-start.9
  145.9 1.9 copy-start.7
  147.5 1.5 copy-start.6
  147.9 1.2 copy-start.8
  149.1 2.1 copy-start.3
  150.5 1.4 copy-start.4
  151.9 42.7 %all-reduce.7.cloned.1.call-start = ((), (), s32[]{:S(2)}) async-start(), calls=%async_computation.4 | async-start | bytes 1572864 | tf_op jit(solution)/shard_map/while/body/eval_jaxpr/psum | solution.py:13
  196.6 42.6 %all-reduce.7.cloned.1.call-start = ((), (), s32[]{:S(2)}) async-start(), calls=%async_computation.4 | async-start | bytes 1572864 | tf_op jit(solution)/shard_map/while/body/eval_jaxpr/psum | solution.py:13
  241.3 42.6 %all-reduce.7.cloned.1.call-start = ((), (), s32[]{:S(2)}) async-start(), calls=%async_computation.4 | async-start | bytes 1572864 | tf_op jit(solution)/shard_map/while/body/eval_jaxpr/psum | solution.py:13
  285.9 25.1 %copy-start.5 = (bf16[3,2,64,1024]{3,0,2,1:T(4,128)(2,1)S(1)}, bf16[3,2,64,1024]{3,0,2,1:T(4,128)(2,1)}, u32[]{:S(2)}) copy-start(bf16[3,2,64,1024]{3,0,2,1:T(4,128)(2,1)} %fusion.35) | copy-start | bytes 2359300
  285.9 196.3 %reduce-scatter.2.cloned.1.call-start = ((), (), s32[]{:S(2)}) async-start(), calls=%async_computation.1 | async-start | bytes 2949120 | tf_op jit(solution)/shard_map/reduce_scatter | solution.py:126
  285.9 26.1 %slice-start = ((s8[4718592]{0:T(1024)(128)(4,1)}), s8[524288]{0:T(1024)(128)(4,1)S(1)}, s32[]{:S(2)}) async-start(s8[4718592]{0:T(1024)(128)(4,1)} %bitcast.81), calls=%async_computation.5 | async-start | bytes 1048576
  311.0 2.2 slice-start.1
  343.7 39.2 %collective-permute-start.1 = (bf16[384,2,1024]{2,0,1:T(8,128)(2,1)S(1)}, bf16[384,2,1024]{2,0,1:T(8,128)(2,1)S(1)}, u32[]{:S(2)}, u32[]{:S(2)}) collective-permute-start(bf16[384,2,1024]{2,0,1:T(8,128)(2,1)S(1)} %fusion.13), channel_id=1, source_target_pairs={{0,1},{1,2},{2,3},{3,0},{4,5},{5,6},{6,7},{7,4},{8,9},{9,10},{10,1... | collective-permute-start | bytes 4718600 | tf_op jit(solution)/shard_map/ppermute | solution.py:102
  343.7 70.5 %collective-permute-start = (bf16[384,2,1024]{2,0,1:T(8,128)(2,1)S(1)}, bf16[384,2,1024]{2,0,1:T(8,128)(2,1)}, u32[]{:S(2)}, u32[]{:S(2)}) collective-permute-start(bf16[384,2,1024]{2,0,1:T(8,128)(2,1)S(1)} %fusion.13), channel_id=1, source_target_pairs={{0,3},{1,0},{2,1},{3,2},{4,7},{5,4},{6,5},{7,6},{8,11},{9,8},{10,9... | collective-permute-start | bytes 4718600 | tf_op jit(solution)/shard_map/ppermute | solution.py:104
  382.8 61.6 %collective-permute-start.2 = (bf16[384,2,1024]{2,0,1:T(8,128)(2,1)S(1)}, bf16[384,2,1024]{2,0,1:T(8,128)(2,1)S(1)}, u32[]{:S(2)}, u32[]{:S(2)}) collective-permute-start(bf16[384,2,1024]{2,0,1:T(8,128)(2,1)S(1)} %collective-permute-done.1), channel_id=1, source_target_pairs={{0,1},{1,2},{2,3},{3,0},{4,5},{5,6},{6,7},{7,4},{8,9},{9,10},{10,1... | collective-permute-start | bytes 4718600 | tf_op jit(solution)/shard_map/ppermute | solution.py:102
  444.5 39.6 %copy-start.1 = (bf16[8,2,64,1024]{3,2,1,0:T(8,128)(2,1)S(1)}, bf16[8,2,64,1024]{3,2,1,0:T(8,128)(2,1)}, u32[]{:S(2)}) copy-start(bf16[8,2,64,1024]{3,2,1,0:T(8,128)(2,1)} %param.23) | copy-start | bytes 6291460
Sparse Core Ops, SparseCore 0:
  8.9 39.7 all-gather.2
  52.6 93.2 all-reduce.4
  159.7 34.7 all-reduce.6
  204.5 34.6 all-reduce.6
  249.1 34.6 all-reduce.6
  451.6 30.6 reduce-scatter.1
